TPU v7x, 32 devices: a whole 2x2x4 slice. The times are simulated.
32 devices in a mesh: dp: 8 (over z, core), tensor: 4 (over y, x).
Axes of the slice: x: 2, y: 2, z: 4, core: 2. Of those that a mesh axis runs over, the one named last changes fastest.
Arguments:
- t_index: int32 [8], P('dp'), may hold values from 0 to 999
- cond_slot: int32 [8], P('dp'), may hold values from 0 to 1
- positions: int32 [8, 3, 512], P('dp'), may hold values from 0 to 63, as said below
- latent: bfloat16 [8, 512, 5120], P('dp', 'tensor'), may hold values from -6 to 6
- teacher_query: bfloat16 [2, 8, 512, 4096], P(None, 'dp', None, 'tensor'), may hold values from -6 to 6
- teacher_key: bfloat16 [2, 8, 512, 4096], P(None, 'dp', None, 'tensor'), may hold values from -6 to 6
- teacher_value: bfloat16 [2, 8, 512, 4096], P(None, 'dp', None, 'tensor'), may hold values from -6 to 6
- student_query: bfloat16 [8, 512, 4096], P('dp', 'tensor'), may hold values from -6 to 6
- student_key: bfloat16 [8, 512, 4096], P('dp', 'tensor'), may hold values from -6 to 6
- student_value: bfloat16 [8, 512, 4096], P('dp', 'tensor'), may hold values from -6 to 6
- query_tangent: bfloat16 [8, 512, 4096], P('dp', 'tensor'), may hold values from -6 to 6
- key_tangent: bfloat16 [8, 512, 4096], P('dp', 'tensor'), may hold values from -6 to 6
- value_tangent: bfloat16 [8, 512, 4096], P('dp', 'tensor'), may hold values from -6 to 6
- teacher_out: bfloat16 [4096, 5120], P('tensor', 'dp'), may hold values from -0.375 to 0.375
- student_out: bfloat16 [4096, 5120], P('tensor', 'dp'), may hold values from -0.375 to 0.375
Outputs:
- target: bfloat16 [8, 512, 5120], P('dp', 'tensor')
- gradient: float32 [4096, 5120], P('tensor', 'dp')
Inputs may be any that keep to these rules, and one draw needn't show every extreme that they name: `positions`: within each clip, tokens 64 m and 64 m + 1 have equal coordinates on all three axes.
All inputs are finite; a program needn't handle non-finite values.
Results may differ from a plain program's by a relative error of at most 0.015.
Values may be sent and summed in bfloat16 or wider, within the bound.
No kernel may reach another device: no remote copies, remote signals or barrier semaphores. Data moves between devices by JAX's collectives and lax.ppermute only.
A program may use at most 192 MiB of HBM per device.

v0:
```python
import math

import jax
import jax.numpy as jnp
from jax import lax
from jax.sharding import PartitionSpec as P

HD = 128
STEPS = 1000


sigma_data = 0.5
guidance = 5.0


def rope_angles(coords):
    half_size = HD // 2
    sixth = HD // 6
    first_pairs = half_size - 2 * sixth
    pair_index = jnp.arange(half_size)
    axis_id = (pair_index >= first_pairs).astype(jnp.int32) + (
        pair_index >= first_pairs + sixth
    ).astype(jnp.int32)
    offset = jnp.where(axis_id == 0, 0, jnp.where(axis_id == 1, first_pairs, first_pairs + sixth))
    axis_width = jnp.where(axis_id == 0, 2 * first_pairs, 2 * sixth)
    exponent = 2.0 * (pair_index - offset).astype(jnp.float32) / axis_width.astype(jnp.float32)
    frequency = jnp.exp(-exponent * math.log(10000.0))
    angles = jnp.zeros((coords.shape[1], half_size), jnp.float32)
    for which_axis in range(3):
        chosen = jnp.where(axis_id == which_axis, frequency, 0.0)
        angles = angles + coords[which_axis].astype(jnp.float32)[:, None] * chosen[None, :]
    return angles


def rotate_heads(source, angles):
    half_size = source.shape[-1] // 2
    cos_angle = jnp.cos(angles)[:, None, :]
    sin_angle = jnp.sin(angles)[:, None, :]
    front_half = source[..., :half_size]
    back_half = source[..., half_size:]
    return jnp.concatenate(
        [
            front_half * cos_angle - back_half * sin_angle,
            back_half * cos_angle + front_half * sin_angle,
        ],
        axis=-1,
    )


def split_heads(source):
    return source.reshape(source.shape[0], -1, HD)


def rotated(source, angles):
    row_count = source.shape[0]
    return (
        rotate_heads(split_heads(source).astype(jnp.float32), angles)
        .astype(jnp.bfloat16)
        .reshape(row_count, -1)
    )


def softmax_rows(scores):
    row_peak = jnp.max(scores, axis=-1, keepdims=True)
    exponent = jnp.exp(scores - row_peak)
    return exponent / jnp.sum(exponent, axis=-1, keepdims=True)


def attend_plain(queries, key_rows, value_rows):
    scores = jnp.einsum(
        "qhd,khd->hqk", queries, key_rows, preferred_element_type=jnp.float32
    ) * HD ** (-0.5)
    rounded = softmax_rows(scores).astype(jnp.bfloat16)
    return jnp.einsum("hqk,khd->qhd", rounded, value_rows, preferred_element_type=jnp.float32)


def attend_tangent(queries, key_rows, value_rows, query_dir, key_dir, value_dir):
    score_scale = HD ** (-0.5)
    scores = (
        jnp.einsum("qhd,khd->hqk", queries, key_rows, preferred_element_type=jnp.float32)
        * score_scale
    )
    weights = softmax_rows(scores)
    rounded = weights.astype(jnp.bfloat16)
    primal = jnp.einsum("hqk,khd->qhd", rounded, value_rows, preferred_element_type=jnp.float32)
    score_dir = (
        jnp.einsum("qhd,khd->hqk", query_dir, key_rows, preferred_element_type=jnp.float32)
        + jnp.einsum("qhd,khd->hqk", queries, key_dir, preferred_element_type=jnp.float32)
    ) * score_scale
    weight_dir = weights * (score_dir - jnp.sum(weights * score_dir, axis=-1, keepdims=True))
    rounded_dir = weight_dir.astype(jnp.bfloat16)
    tangent = jnp.einsum(
        "hqk,khd->qhd", rounded_dir, value_rows, preferred_element_type=jnp.float32
    ) + jnp.einsum("hqk,khd->qhd", rounded, value_dir, preferred_element_type=jnp.float32)
    return (primal, tangent)


def local(
    t_index,
    cond_slot,
    positions,
    latent,
    teacher_query,
    teacher_key,
    teacher_value,
    student_query,
    student_key,
    student_value,
    query_tangent,
    key_tangent,
    value_tangent,
    teacher_out,
    student_out,
):
    groups = lax.axis_size("tensor")
    seq_local = latent.shape[1]
    seq_whole = seq_local * groups
    row_start = lax.axis_index("tensor") * seq_local
    time_value = 0.2 + 1.2 * (t_index[0].astype(jnp.float32) + 0.5) / STEPS
    cos_time = jnp.cos(time_value)
    sin_time = jnp.sin(time_value)
    angles_whole = rope_angles(positions[0])
    angles_local = lax.dynamic_slice_in_dim(angles_whole, row_start, seq_local, 0)
    outgoing = (
        rotated(student_query[0], angles_local),
        rotated(student_key[0], angles_local),
        student_value[0],
        rotated(query_tangent[0], angles_local),
        rotated(key_tangent[0], angles_local),
        value_tangent[0],
    )
    arrived = (
        lax.all_to_all(outgoing[0], "tensor", split_axis=1, concat_axis=0, tiled=True),
        lax.all_to_all(outgoing[1], "tensor", split_axis=1, concat_axis=0, tiled=True),
        lax.all_to_all(outgoing[2], "tensor", split_axis=1, concat_axis=0, tiled=True),
        lax.all_to_all(outgoing[3], "tensor", split_axis=1, concat_axis=0, tiled=True),
        lax.all_to_all(outgoing[4], "tensor", split_axis=1, concat_axis=0, tiled=True),
        lax.all_to_all(outgoing[5], "tensor", split_axis=1, concat_axis=0, tiled=True),
    )
    outputs = []
    for stream in range(2):
        outputs.append(
            attend_plain(
                split_heads(rotated(teacher_query[stream, 0], angles_whole)),
                split_heads(rotated(teacher_key[stream, 0], angles_whole)),
                split_heads(teacher_value[stream, 0]),
            )
        )
    cond_index = cond_slot[0]
    cond_out = jnp.where(cond_index == 0, outputs[0], outputs[1])
    uncond_out = jnp.where(cond_index == 0, outputs[1], outputs[0])
    teacher_term = (
        (cos_time * cos_time * sigma_data * (uncond_out + guidance * (cond_out - uncond_out)))
        .astype(jnp.bfloat16)
        .reshape(seq_whole, -1)
    )
    primal, tangent = attend_tangent(
        split_heads(arrived[0]),
        split_heads(arrived[1]),
        split_heads(arrived[2]),
        split_heads(arrived[3]),
        split_heads(arrived[4]),
        split_heads(arrived[5]),
    )
    student_term = (
        (-(cos_time * cos_time) * sigma_data * primal - cos_time * sin_time * sigma_data * tangent)
        .astype(jnp.bfloat16)
        .reshape(seq_whole, -1)
    )
    attended = primal.astype(jnp.bfloat16).reshape(seq_whole, -1)
    stacked = jnp.stack([student_out, teacher_out])
    pieces = lax.all_gather(stacked, "dp", axis=2, tiled=True)
    partial_value = jnp.dot(student_term, pieces[0], preferred_element_type=jnp.float32) + jnp.dot(
        teacher_term, pieces[1], preferred_element_type=jnp.float32
    )
    latent_weight = cos_time * sin_time
    velocity = lax.psum_scatter(
        partial_value.astype(jnp.bfloat16), "tensor", scatter_dimension=0, tiled=True
    ).astype(jnp.float32)
    target = (velocity - latent_weight * latent[0].astype(jnp.float32)).astype(jnp.bfloat16)
    contracted = lax.dot_general(
        attended,
        lax.all_gather(target, "tensor", axis=0, tiled=True),
        (((0,), (0,)), ((), ())),
        preferred_element_type=jnp.float32,
    )
    grad_scale = -2.0 / math.sqrt(lax.axis_size("dp") * seq_whole)
    gradient = lax.psum_scatter(
        (grad_scale * contracted).astype(jnp.bfloat16), "dp", scatter_dimension=1, tiled=True
    ).astype(jnp.float32)
    return (target[None], gradient)


def solution(mesh):
    placed = (
        P("dp"),
        P("dp"),
        P("dp", None, None),
        P("dp", "tensor", None),
        P(None, "dp", None, "tensor"),
        P(None, "dp", None, "tensor"),
        P(None, "dp", None, "tensor"),
        P("dp", "tensor", None),
        P("dp", "tensor", None),
        P("dp", "tensor", None),
        P("dp", "tensor", None),
        P("dp", "tensor", None),
        P("dp", "tensor", None),
        P("tensor", "dp"),
        P("tensor", "dp"),
    )
    return jax.shard_map(
        local,
        mesh=mesh,
        in_specs=placed,
        out_specs=(P("dp", "tensor", None), P("tensor", "dp")),
        check_vma=False,
    )
```

profile of v0, /device:TPU:0, one launch (start us, length us, event | category | flops | bytes accessed | tf_op | source)
XLA Modules:
  0.0 546.2 jit_solution(1457230556964444309)
XLA Ops:
  7.2 3.6 pad_maximum_fusion
  19.6 6.6 %subtract_convert_fusion.5 = (bf16[128,32,64]{0,2,1:T(8,128)(2,1)}, bf16[128,32,64]{0,2,1:T(8,128)(2,1)}, bf16[128,32,64]{0,2,1:T(8,128)(2,1)}, bf16[128,32,64]{...) fusion(f32[128,32,128]{0,2,1:T(8,128)} %bitcast.103, ...), kind=kLoop, calls=%fused_computation.74 | loop fusion | flops 8388608 | bytes 12648448 | tf_op jit(solution)/shard_map/convert.16
  27.3 5.2 all-to-all-start
  52.5 3.3 copy.179
  62.7 4.2 all-to-all-start.1
  71.7 3.2 copy.183
  78.0 3.2 copy.185
  81.2 3.2 copy.186
  87.8 4.2 all-to-all-start.3
  92.0 8.8 %subtract_convert_fusion = (bf16[512,8,64]{2,0,1:T(8,128)(2,1)S(1)}, bf16[512,8,64]{2,0,1:T(8,128)(2,1)}, bf16[512,8,64]{2,0,1:T(8,128)(2,1)}, bf16[512,8,64]{2,...) fusion(f32[512,8,64]{2,0,1:T(8,128)} %copy.186, ...), kind=kLoop, calls=%fused_computation.40 | loop fusion | flops 8388608 | bytes 12845056 | tf_op jit(solution)/shard_map/convert.8
  100.8 5.4 all-to-all-done.3
  106.2 16.4 %all-to-all-start.4 = ((bf16[128,4,1024]{0,2,1:T(8,128)(2,1)}), bf16[128,4,1024]{0,2,1:T(8,128)(2,1)}, u32[]{:S(2)}, u32[]{:S(2)}) async-start(bf16[128,4,1024]{0,2,1:T(8,128)(2,1)} %bitcast.110), calls=%async_computation.4 | async-start | bytes 2097152 | tf_op jit(solution)/shard_map/all_to_all | solution.py:137
  122.6 3.7 fusion.30
  126.3 3.3 copy-done.2
  131.9 3.9 all-to-all-done.4
  135.8 4.3 all-to-all-start.2
  148.0 5.3 all-to-all-done.2
  153.3 4.2 all-to-all-start.5
  161.9 10.3 %fusion.19 = f32[8,512,128]{1,2,0:T(8,128)} fusion(bf16[512,8,128]{0,2,1:T(8,128)(2,1)S(1)} %bitcast.122, f32[8,512]{1,0:T(8,128)S(1)} %fusion.97, f32[8,512,512]{1,2,0:T(8,128)} %copy-done.2), kind=kOutput, calls=%fused_computation.29 | convolution fusion | flops 547361280 | bytes 11550720 | tf_op jit(solution)/shard_map/hqk,khd->qhd/dot_general | solution.py:74
  172.2 10.8 %fusion.25 = bf16[512,8,128]{0,2,1:T(8,128)(2,1)} fusion(f32[8,512,128]{1,2,0:T(8,128)} %fusion.19, f32[]{:T(128)} %bitcast.26, pred[]{:T(512)} %bitcast.27, bf16[512,8,128]{0,2,1:T(8,128)(2,1)S(1)} %bitcast.121, f32[8,512]{1,0:T(8,128)S(1)} %fusion.98, f32[8,512,512]{1,2,0:T(8,128)} %copy-done.3), kind=kOutput, calls=%fused_computation.38 | convolution fusion | flops 551031296 | bytes 12599301 | tf_op jit(solution)/shard_map/hqk,khd->qhd/dot_general | solution.py:74
  207.0 5.5 %fusion.99 = (f32[8,512]{1,0:T(8,128)S(1)}, f32[8,512,512]{1,2,0:T(8,128)}) fusion(f32[8,512,512]{1,2,0:T(8,128)S(1)} %fusion.48), kind=kOutput, calls=%fused_computation.125 | output fusion | flops 8389119 | bytes 16793600 | tf_op jit(solution)/shard_map/sub | solution.py:65
  213.0 10.4 %fusion.28 = f32[8,512,128]{1,2,0:T(8,128)} fusion(bf16[512,8,128]{0,2,1:T(8,128)(2,1)} %reshape.309, f32[8,512]{1,0:T(8,128)S(1)} %get-tuple-element.52, f32[8,512,512]{1,2,0:T(8,128)} %copy-done), kind=kOutput, calls=%fused_computation.50 | convolution fusion | flops 547361280 | bytes 11550720 | tf_op jit(solution)/shard_map/hqk,khd->qhd/dot_general | solution.py:94
  223.4 10.8 %fusion.100 = (bf16[8,512,128]{1,2,0:T(8,128)(2,1)}, f32[8,512,128]{1,2,0:T(8,128)}) fusion(bf16[512,8,128]{0,2,1:T(8,128)(2,1)} %reshape.306, f32[8,512]{1,0:T(8,128)S(1)} %get-tuple-element.52, f32[8,512,512]{1,2,0:T(8,128)} %copy-done), kind=kOutput, calls=%fused_computation.126 | convolution fusion | flops 547885568 | bytes 12599296 | tf_op jit(solution)/shard_map/hqk,khd->qhd/dot_general | solution.py:85
  237.7 4.3 multiply_reduce_fusion
  242.1 11.3 %subtract_convert_fusion.4 = bf16[8,512,128]{1,2,0:T(8,128)(2,1)S(1)} fusion(f32[8,512,128]{1,2,0:T(8,128)} %fusion.28, f32[8,512,128]{1,2,0:T(8,128)} %get-tuple-element.57, bf16[512,8,128]{0,2,1:T(8,128)(2,1)S(1)} %copy-done.12, f32[8,512,512]{1,2,0:T(8,128)} %get-tuple-element.55, f32[8,512]{1,0:T(8,128)S(1)} %get-tuple-element.54, f32[]{:T(128)S(6)} %mul.409, ...), kind=kOutput, calls=%fused_computation.47 | convolution fusion | flops 554177024 | bytes 23101448 | tf_op jit(solution)/shard_map/hqk,khd->qhd/dot_general | solution.py:92
  253.4 8.5 %fusion.3 = f32[512,5120]{1,0:T(8,128)S(1)} fusion(bf16[512,1024]{0,1:T(8,128)(2,1)S(1)} %bitcast.116, bf16[2,1024,5120]{2,1,0:T(8,128)(2,1)} %all-gather.3.cloned.1.call-done), kind=kOutput, calls=%fused_computation.5 | convolution fusion | flops 5368709120 | bytes 22020096 | tf_op jit(solution)/shard_map/dot_general | solution.py:173
  262.0 11.9 %add_convert_fusion = bf16[512,5120]{1,0:T(8,128)(2,1)} fusion(f32[512,5120]{1,0:T(8,128)S(1)} %fusion.3, bf16[512,1024]{0,1:T(8,128)(2,1)S(1)} %bitcast.123, bf16[2,1024,5120]{2,1,0:T(8,128)(2,1)} %all-gather.3.cloned.1.call-done), kind=kOutput, calls=%fused_computation.8 | convolution fusion | flops 5373952000 | bytes 27262976 | tf_op jit(solution)/shard_map/dot_general | solution.py:173
  273.9 63.2 %reduce-scatter.5.cloned.1.call-done = bf16[128,5120]{1,0:T(8,128)(2,1)} async-done(((bf16[512,5120]{1,0:T(8,128)(2,1)}), bf16[128,5120]{1,0:T(8,128)(2,1)}) %reduce-scatter.5.cloned.1.call-update) | async-done | bytes 1310736 | tf_op jit(solution)/shard_map/reduce_scatter | solution.py:177
  340.0 61.5 %all-gather.5.cloned.1.call-done = bf16[512,5120]{1,0:T(8,128)(2,1)} async-done(((bf16[128,5120]{1,0:T(8,128)(2,1)}), bf16[512,5120]{1,0:T(8,128)(2,1)}) %all-gather.5.cloned.1.call-update) | async-done | bytes 5242896 | tf_op jit(solution)/shard_map/all_gather | solution.py:183
  401.5 10.6 %multiply_convert_fusion = bf16[1024,5120]{1,0:T(8,128)(2,1)} fusion(bf16[512,1024]{0,1:T(8,128)(2,1)S(1)} %bitcast.127, bf16[512,5120]{1,0:T(8,128)(2,1)} %all-gather.5.cloned.1.call-done), kind=kOutput, calls=%fused_computation.3 | convolution fusion | flops 5379194880 | bytes 16777216 | tf_op jit(solution)/shard_map/dot_general | solution.py:181
  412.1 14.4 %copy.173 = bf16[1024,5120]{0,1:T(8,128)(2,1)} copy(bf16[1024,5120]{1,0:T(8,128)(2,1)} %multiply_convert_fusion) | data formatting | bytes 20971520
  426.6 109.6 %reduce-scatter.7.cloned.1.call-done = bf16[640,1024]{1,0:T(8,128)(2,1)} async-done(((bf16[5120,1024]{1,0:T(8,128)(2,1)}), bf16[640,1024]{1,0:T(8,128)(2,1)}) %reduce-scatter.7.cloned.1.call-update) | async-done | bytes 1310736
  (99 shorter events, 95.3 us)
Async XLA Ops:
  7.2 3.6 copy-start.10
  7.2 246.2 %all-gather.3.cloned.1.call-start = ((), (), s32[]{:S(2)}) async-start(), calls=%async_computation.8 | async-start | bytes 23592960 | tf_op jit(solution)/shard_map/all_gather | solution.py:172
  11.3 5.2 copy-start.11
  11.4 6.9 %copy-start.15 = (s32[1,3,512]{2,0,1:T(1,128)S(1)}, s32[1,3,512]{2,0,1:T(1,128)}, u32[]{:S(2)}) copy-start(s32[1,3,512]{2,0,1:T(1,128)} %param.17) | copy-start | bytes 18436
  27.3 35.4 %all-to-all-start = ((bf16[128,4,1024]{0,2,1:T(8,128)(2,1)}), bf16[128,4,1024]{0,2,1:T(8,128)(2,1)}, u32[]{:S(2)}, u32[]{:S(2)}) async-start(bf16[128,4,1024]{0,2,1:T(8,128)(2,1)} %bitcast.5), calls=%async_computation | async-start | bytes 2097152 | tf_op jit(solution)/shard_map/all_to_all | solution.py:133
  35.7 5.8 %copy-start.14 = (f32[512,64]{0,1:T(8,128)S(1)}, f32[512,64]{0,1:T(8,128)}, u32[]{:S(2)}) copy-start(f32[512,64]{0,1:T(8,128)} %get-tuple-element.47) | copy-start | bytes 393220
  62.7 25.1 %all-to-all-start.1 = ((bf16[128,4,1024]{0,2,1:T(8,128)(2,1)}), bf16[128,4,1024]{0,2,1:T(8,128)(2,1)}, u32[]{:S(2)}, u32[]{:S(2)}) async-start(bf16[128,4,1024]{0,2,1:T(8,128)(2,1)} %bitcast.111), calls=%async_computation.1 | async-start | bytes 2097152 | tf_op jit(solution)/shard_map/all_to_all | solution.py:134
  78.0 8.7 %copy-start.6 = (bf16[128,32,64]{0,2,1:T(8,128)(2,1)S(1)}, bf16[128,32,64]{0,2,1:T(8,128)(2,1)}, u32[]{:S(2)}) copy-start(bf16[128,32,64]{0,2,1:T(8,128)(2,1)} %get-tuple-element.10) | copy-start | bytes 1572868
  78.0 8.7 %copy-start.7 = (bf16[128,32,64]{0,2,1:T(8,128)(2,1)S(1)}, bf16[128,32,64]{0,2,1:T(8,128)(2,1)}, u32[]{:S(2)}) copy-start(bf16[128,32,64]{0,2,1:T(8,128)(2,1)} %get-tuple-element.11) | copy-start | bytes 1572868
  87.8 18.5 %all-to-all-start.3 = ((bf16[128,4,1024]{0,2,1:T(8,128)(2,1)}), bf16[128,4,1024]{0,2,1:T(8,128)(2,1)}, u32[]{:S(2)}, u32[]{:S(2)}) async-start(bf16[128,4,1024]{0,2,1:T(8,128)(2,1)} %bitcast.14), calls=%async_computation.3 | async-start | bytes 2097152 | tf_op jit(solution)/shard_map/all_to_all | solution.py:136
  106.2 29.5 %all-to-all-start.4 = ((bf16[128,4,1024]{0,2,1:T(8,128)(2,1)}), bf16[128,4,1024]{0,2,1:T(8,128)(2,1)}, u32[]{:S(2)}, u32[]{:S(2)}) async-start(bf16[128,4,1024]{0,2,1:T(8,128)(2,1)} %bitcast.110), calls=%async_computation.4 | async-start | bytes 2097152 | tf_op jit(solution)/shard_map/all_to_all | solution.py:137
  126.3 3.3 copy-start.2
  129.6 10.4 %copy-start.4 = (bf16[512,8,64]{2,0,1:T(8,128)(2,1)S(1)}, bf16[512,8,64]{2,0,1:T(8,128)(2,1)}, u32[]{:S(2)}) copy-start(bf16[512,8,64]{2,0,1:T(8,128)(2,1)} %get-tuple-element.3) | copy-start | bytes 1572868
  129.6 10.4 %copy-start.5 = (bf16[512,8,64]{2,0,1:T(8,128)(2,1)S(1)}, bf16[512,8,64]{2,0,1:T(8,128)(2,1)}, u32[]{:S(2)}) copy-start(bf16[512,8,64]{2,0,1:T(8,128)(2,1)} %get-tuple-element.34) | copy-start | bytes 1572868
  135.8 17.6 %all-to-all-start.2 = ((bf16[128,4,1024]{0,2,1:T(8,128)(2,1)}), bf16[128,4,1024]{0,2,1:T(8,128)(2,1)}, u32[]{:S(2)}, u32[]{:S(2)}) async-start(bf16[128,4,1024]{0,2,1:T(8,128)(2,1)} %bitcast.109), calls=%async_computation.2 | async-start | bytes 2097152 | tf_op jit(solution)/shard_map/all_to_all | solution.py:135
  142.6 3.2 copy-start.3
  153.3 47.1 %all-to-all-start.5 = ((bf16[128,4,1024]{0,2,1:T(8,128)(2,1)}), bf16[128,4,1024]{0,2,1:T(8,128)(2,1)}, u32[]{:S(2)}, u32[]{:S(2)}) async-start(bf16[128,4,1024]{0,2,1:T(8,128)(2,1)} %bitcast.19), calls=%async_computation.5 | async-start | bytes 2097152 | tf_op jit(solution)/shard_map/all_to_all | solution.py:138
  157.6 179.6 %reduce-scatter.5.cloned.1.call-start = ((), (), s32[]{:S(2)}) async-start(), calls=%async_computation.9 | async-start | bytes 6553600 | tf_op jit(solution)/shard_map/reduce_scatter | solution.py:177
  207.0 6.0 %copy-start = (f32[8,512,512]{1,2,0:T(8,128)}, f32[8,512,512]{1,2,0:T(8,128)S(1)}, u32[]{:S(2)}) copy-start(f32[8,512,512]{1,2,0:T(8,128)S(1)} %fusion.48) | copy-start | bytes 25165828
  234.1 3.4 copy-start.1
  234.1 3.6 copy-start.13
  237.7 4.3 copy-start.12
  242.1 11.3 %copy-start.8 = (bf16[512,8,128]{0,2,1:T(8,128)(2,1)S(1)}, bf16[512,8,128]{0,2,1:T(8,128)(2,1)}, u32[]{:S(2)}) copy-start(bf16[512,8,128]{0,2,1:T(8,128)(2,1)} %fusion.25) | copy-start | bytes 3145732
  273.9 63.3 %copy-start.9 = (bf16[1,128,5120]{2,1,0:T(8,128)(2,1)S(1)}, bf16[1,128,5120]{2,1,0:T(8,128)(2,1)}, u32[]{:S(2)}) copy-start(bf16[1,128,5120]{2,1,0:T(8,128)(2,1)} %param.18) | copy-start | bytes 3932164
  273.9 127.6 %copy-start.16 = (bf16[8,512,128]{1,2,0:T(8,128)(2,1)S(1)}, bf16[8,512,128]{1,2,0:T(8,128)(2,1)}, u32[]{:S(2)}) copy-start(bf16[8,512,128]{1,2,0:T(8,128)(2,1)} %get-tuple-element.56) | copy-start | bytes 3145732
  273.9 127.6 %all-gather.5.cloned.1.call-start = ((), (), s32[]{:S(2)}) async-start(), calls=%async_computation.10 | async-start | bytes 6553600 | tf_op jit(solution)/shard_map/all_gather | solution.py:183
  339.9 196.2 %reduce-scatter.7.cloned.1.call-start = ((), (), s32[]{:S(2)}) async-start(), calls=%async_computation.11 | async-start | bytes 11796480
Sparse Core Ops, SparseCore 0:
  10.9 188.0 all-gather.2
  274.0 63.0 reduce-scatter.4
  340.0 61.4 all-gather.4
  426.7 109.4 reduce-scatter.6
where the time goes:
time: 550 us; the launch traced here: 546 us
  waiting for transfers between devices  249 us (45%)
  local copies, waits for them, and re-layouts  104 us (19%)
  matrix products  97.7 us (18%)
  other arithmetic  41.2 us (7%)
  starting transfers between devices  38.7 us (7%)
  between operations  15.8 us (3%)
    unnamed x5, waiting for transfers between devices  110 us
    reduce_scatter x1, waiting for transfers between devices, local(): lax.psum_scatter(partial_value.astype(jnp.bfloat16), 'tensor', scatter_di...  63.2 us
    unnamed x54, local copies, waits for them, and re-layouts  62.5 us
    all_gather x1, waiting for transfers between devices, local(): lax.all_gather(target, 'tensor', axis=0, tiled=True)  61.5 us
    dot_general x2, matrix products, attend_plain(): jnp.einsum('hqk,khd->qhd', rounded, value_rows, preferred_element_type=jn...  21.1 us
    all_to_all x1, starting transfers between devices, local(): lax.all_to_all(outgoing[4], 'tensor', split_axis=1, concat_axis=0, tiled=...  16.4 us
    another operation x2, other arithmetic  15.3 us
    dot_general x1, matrix products, local(): jnp.dot(student_term, pieces[0], preferred_element_type=jnp.float32)  11.9 us
  transfers between devices with their start and end apart: 10, of which 6 were waited for; matrix products, arithmetic and copies ran while one was open for 33% of the time, Pallas kernels for 0%

commit v1 on v0

--- a/solution.py
+++ b/solution.py
@@ -174,20 +174,26 @@
         teacher_term, pieces[1], preferred_element_type=jnp.float32
     )
     latent_weight = cos_time * sin_time
+    clips = lax.axis_size("dp")
+    copies = jnp.broadcast_to(attended[None], (clips,) + attended.shape)
+    attended_all = lax.all_to_all(copies, "dp", split_axis=0, concat_axis=0, tiled=True)
     velocity = lax.psum_scatter(
         partial_value.astype(jnp.bfloat16), "tensor", scatter_dimension=0, tiled=True
-    ).astype(jnp.float32)
-    target = (velocity - latent_weight * latent[0].astype(jnp.float32)).astype(jnp.bfloat16)
-    contracted = lax.dot_general(
-        attended,
-        lax.all_gather(target, "tensor", axis=0, tiled=True),
-        (((0,), (0,)), ((), ())),
-        preferred_element_type=jnp.float32,
-    )
-    grad_scale = -2.0 / math.sqrt(lax.axis_size("dp") * seq_whole)
-    gradient = lax.psum_scatter(
-        (grad_scale * contracted).astype(jnp.bfloat16), "dp", scatter_dimension=1, tiled=True
-    ).astype(jnp.float32)
+    )
+    velocity, attended_all = lax.optimization_barrier((velocity, attended_all))
+    target = (
+        velocity.astype(jnp.float32) - latent_weight * latent[0].astype(jnp.float32)
+    ).astype(jnp.bfloat16)
+    width = target.shape[1] // clips
+    columns = lax.all_to_all(
+        target.reshape(seq_local, clips, width), "dp", split_axis=1, concat_axis=1, tiled=True
+    )
+    columns = lax.all_gather(columns, "tensor", axis=0, tiled=True)
+    grad_scale = -2.0 / math.sqrt(clips * seq_whole)
+    terms = jnp.einsum(
+        "csi,scd->cid", attended_all, columns, preferred_element_type=jnp.float32
+    )
+    gradient = jnp.sum((grad_scale * terms).astype(jnp.bfloat16).astype(jnp.float32), axis=0)
     return (target[None], gradient)
 
 

time: 550 us -> 532 us (0.967)
  waiting for transfers between devices: 249 us -> 200 us
  blocking collectives: 0 us -> 35.4 us
  local copies, waits for them, and re-layouts: 104 us -> 85.2 us
  matrix products: 97.7 us -> 112 us
  starting transfers between devices: 38.7 us -> 32.9 us
    all_to_all x0 -> x1, waiting for transfers between devices: none -> 129 us  [local(): lax.all_to_all(copies, 'dp', split_axis=0, concat_axis=0, tiled=True)]
    unnamed x5 -> x3, waiting for transfers between devices: 110 us -> 0.05 us
    reduce_scatter x1, waiting for transfers between devices: 63.2 us -> 0.01 us  [local(): lax.psum_scatter(partial_value.astype(jnp.bfloat16), 'tensor', scatter_di...]
    all_to_all x0 -> x1, blocking collectives: none -> 35.4 us  [local(): lax.all_to_all(target.reshape(seq_local, clips, width), 'dp', split_axis=...]
    unnamed x54, local copies, waits for them, and re-layouts: 62.5 us -> 40.8 us
    all_to_all x1, starting transfers between devices: 16.4 us -> 4.28 us  [local(): lax.all_to_all(outgoing[4], 'tensor', split_axis=1, concat_axis=0, tiled=...]
    dot_general x1, matrix products: 4.31 us -> 9.94 us  [attend_tangent(): jnp.einsum('qhd,khd->hqk', queries, key_dir, preferred_element_type=jnp.f...]
  transfers between devices with their start and end apart: 10 -> 10, of which waited for: 6 -> 4; matrix products, arithmetic and copies ran while one was open for 33% -> 41% of each run, Pallas kernels for 0% -> 0%
where the time goes in v1:
time: 532 us; the launch traced here: 523 us
  waiting for transfers between devices  200 us (38%)
  matrix products  112 us (21%)
  local copies, waits for them, and re-layouts  85.2 us (16%)
  other arithmetic  42 us (8%)
  blocking collectives  35.4 us (7%)
  starting transfers between devices  32.9 us (6%)
  between operations  15.8 us (3%)
    all_to_all x1, waiting for transfers between devices, local(): lax.all_to_all(copies, 'dp', split_axis=0, concat_axis=0, tiled=True)  129 us
    all_gather x1, waiting for transfers between devices, local(): columns = lax.all_gather(columns, 'tensor', axis=0, tiled=True)  61 us
    unnamed x54, local copies, waits for them, and re-layouts  40.8 us
    all_to_all x1, blocking collectives, local(): lax.all_to_all(target.reshape(seq_local, clips, width), 'dp', split_axis=...  35.4 us
    dot_general x2, matrix products, attend_plain(): jnp.einsum('hqk,khd->qhd', rounded, value_rows, preferred_element_type=jn...  21 us
    another operation x2, other arithmetic  15.4 us
    sub x3, other arithmetic, softmax_rows(): exponent = jnp.exp(scores - row_peak)  15.2 us
    dot_general x1, matrix products, local(): jnp.einsum('csi,scd->cid', attended_all, columns, preferred_element_type=...  12.3 us
  transfers between devices with their start and end apart: 10, of which 4 were waited for; matrix products, arithmetic and copies ran while one was open for 41% of the time, Pallas kernels for 0%

profile of v1, /device:TPU:0, one launch (start us, length us, event | category | flops | bytes accessed | tf_op | source)
XLA Modules:
  0.0 523.3 jit_solution(12055977299198744937)
XLA Ops:
  7.2 3.6 pad_maximum_fusion
  19.1 6.6 %subtract_convert_fusion.5 = (bf16[128,32,64]{0,2,1:T(8,128)(2,1)}, bf16[128,32,64]{0,2,1:T(8,128)(2,1)}, bf16[128,32,64]{0,2,1:T(8,128)(2,1)}, bf16[128,32,64]{...) fusion(f32[128,32,128]{0,2,1:T(8,128)} %bitcast.104, ...), kind=kLoop, calls=%fused_computation.76 | loop fusion | flops 8388608 | bytes 12648448 | tf_op jit(solution)/shard_map/convert.16
  26.7 5.3 %all-to-all-start = ((bf16[128,4,1024]{0,2,1:T(8,128)(2,1)}), bf16[128,4,1024]{0,2,1:T(8,128)(2,1)}, u32[]{:S(2)}, u32[]{:S(2)}) async-start(bf16[128,4,1024]{0,2,1:T(8,128)(2,1)} %bitcast.5), calls=%async_computation | async-start | bytes 2097152 | tf_op jit(solution)/shard_map/all_to_all | solution.py:133
  49.1 3.2 copy.182
  52.3 3.2 copy.183
  77.9 4.2 all-to-all-start.1
  82.2 8.8 %subtract_convert_fusion = (bf16[512,8,64]{2,0,1:T(8,128)(2,1)S(1)}, bf16[512,8,64]{2,0,1:T(8,128)(2,1)}, bf16[512,8,64]{2,0,1:T(8,128)(2,1)}, bf16[512,8,64]{2,...) fusion(f32[512,8,64]{2,0,1:T(8,128)} %copy.189, ...), kind=kLoop, calls=%fused_computation.41 | loop fusion | flops 8388608 | bytes 12845056 | tf_op jit(solution)/shard_map/convert.8
  90.9 5.4 %all-to-all-done.1 = bf16[128,4,1024]{0,2,1:T(8,128)(2,1)} async-done(((bf16[128,4,1024]{0,2,1:T(8,128)(2,1)}), bf16[128,4,1024]{0,2,1:T(8,128)(2,1)}, u32[]{:S(2)}, u32[]{:S(2)}) %all-to-all-start.1) | async-done | bytes 1048608 | tf_op jit(solution)/shard_map/all_to_all | solution.py:134
  96.3 4.4 all-to-all-start.3
  100.8 6.9 %fusion.30 = f32[8,512,512]{1,2,0:T(8,128)} fusion(bf16[512,8,64]{2,0,1:T(8,128)(2,1)} %get-tuple-element.40, bf16[512,8,64]{2,0,1:T(8,128)(2,1)} %get-tuple-element.41, bf16[512,8,64]{2,0,1:T(8,128)(2,1)} %get-tuple-element.36, bf16[512,8,64]{2,0,1:T(8,128)(2,1)} %get-tuple-element.37), kind=kOutput, calls=%fused_computation.58 | convolution fusion | flops 541065216 | bytes 10485760 | tf_op jit(solution)/shard_map/qhd,khd->hqk/dot_general | solution.py:70
  110.2 8.0 %fusion.97 = f32[8,512]{1,0:T(8,128)S(1)} fusion(f32[8,512,512]{1,2,0:T(8,128)} %fusion.30), kind=kOutput, calls=%fused_computation.125 | output fusion | flops 8389119 | bytes 8404992 | tf_op jit(solution)/shard_map/sub | solution.py:65
  118.2 4.3 all-to-all-start.4
  125.2 3.3 copy-done.1
  130.7 5.1 all-to-all-done.4
  135.8 4.5 all-to-all-start.2
  145.9 10.2 %fusion.19 = f32[8,512,128]{1,2,0:T(8,128)} fusion(bf16[512,8,128]{0,2,1:T(8,128)(2,1)S(1)} %bitcast.125, f32[8,512]{1,0:T(8,128)S(1)} %fusion.97, f32[8,512,512]{1,2,0:T(8,128)} %fusion.30), kind=kOutput, calls=%fused_computation.30 | convolution fusion | flops 547361280 | bytes 11550720 | tf_op jit(solution)/shard_map/hqk,khd->qhd/dot_general | solution.py:74
  156.1 10.8 %fusion.25 = bf16[512,8,128]{0,2,1:T(8,128)(2,1)} fusion(f32[8,512,128]{1,2,0:T(8,128)} %fusion.19, f32[]{:T(128)} %bitcast.26, pred[]{:T(512)} %bitcast.27, bf16[512,8,128]{0,2,1:T(8,128)(2,1)S(1)} %bitcast.124, f32[8,512]{1,0:T(8,128)S(1)} %fusion.98, f32[8,512,512]{1,2,0:T(8,128)} %copy-done.1), kind=kOutput, calls=%fused_computation.39 | convolution fusion | flops 551031296 | bytes 12599301 | tf_op jit(solution)/shard_map/hqk,khd->qhd/dot_general | solution.py:74
  179.0 4.7 all-to-all-start.5
  190.3 5.0 fusion.99
  196.2 10.9 %fusion.100 = (bf16[8,512,128]{1,2,0:T(8,128)(2,1)}, f32[8,512,128]{1,2,0:T(8,128)}) fusion(bf16[512,8,128]{0,2,1:T(8,128)(2,1)} %reshape.307, f32[8,512]{1,0:T(8,128)S(1)} %get-tuple-element.56, f32[8,512,512]{1,2,0:T(8,128)} %copy-done), kind=kOutput, calls=%fused_computation.128 | convolution fusion | flops 547885568 | bytes 12599296 | tf_op jit(solution)/shard_map/hqk,khd->qhd/dot_general | solution.py:85
  207.2 4.5 fusion.45
  211.7 5.3 %broadcast_in_dim.28 = bf16[8,512,1024]{1,2,0:T(8,128)(2,1)} broadcast(bf16[512,1024]{0,1:T(8,128)(2,1)} %bitcast.122), dimensions={1,2} | broadcast | bytes 9437184 | tf_op jit(solution)/shard_map/broadcast_in_dim | solution.py:178
  217.0 5.1 all-to-all-start.6
  222.2 9.9 %multiply_reduce_fusion = (f32[8,512]{1,0:T(8,128)S(1)}, f32[8,512,512]{1,2,0:T(8,128)}) fusion(f32[8,512,512]{1,2,0:T(8,128)} %get-tuple-element.57, f32[8,512]{1,0:T(8,128)S(1)} %get-tuple-element.56, f32[8,512,512]{1,2,0:T(8,128)} %fusion.45, bf16[512,8,128]{2,1,0:T(8,128)(2,1)S(1)} %bitcast.123, bf16[512,8,128]{2,1,0:T(8,128)(2,1)S(1)} %bitcast.110), kind=kOutput, calls=%fused_computation.15 | convolution fusion | flops 547352576 | bytes 27295744 | tf_op jit(solution)/shard_map/qhd,khd->hqk/dot_general | solution.py:88
  234.6 10.2 %fusion.28 = f32[8,512,128]{1,2,0:T(8,128)} fusion(bf16[512,8,128]{0,2,1:T(8,128)(2,1)S(1)} %reshape.310, f32[8,512]{1,0:T(8,128)S(1)} %get-tuple-element.56, f32[8,512,512]{1,2,0:T(8,128)} %copy-done), kind=kOutput, calls=%fused_computation.51 | convolution fusion | flops 547361280 | bytes 11550720 | tf_op jit(solution)/shard_map/hqk,khd->qhd/dot_general | solution.py:94
  244.8 11.5 %subtract_convert_fusion.4 = bf16[8,512,128]{1,2,0:T(8,128)(2,1)S(1)} fusion(f32[8,512,128]{1,2,0:T(8,128)} %fusion.28, f32[8,512,128]{1,2,0:T(8,128)} %get-tuple-element.61, bf16[512,8,128]{0,2,1:T(8,128)(2,1)S(1)} %copy-done.16, f32[8,512,512]{1,2,0:T(8,128)} %get-tuple-element.59, f32[8,512]{1,0:T(8,128)S(1)} %get-tuple-element.58, f32[]{:T(128)S(6)} %mul.409, ...), kind=kOutput, calls=%fused_computation.48 | convolution fusion | flops 554177024 | bytes 23101448 | tf_op jit(solution)/shard_map/hqk,khd->qhd/dot_general | solution.py:92
  256.4 8.4 %fusion.3 = f32[512,5120]{1,0:T(8,128)S(1)} fusion(bf16[512,1024]{0,1:T(8,128)(2,1)S(1)} %bitcast.119, bf16[2,1024,5120]{2,1,0:T(8,128)(2,1)} %all-gather.3.cloned.1.call-done), kind=kOutput, calls=%fused_computation.6 | convolution fusion | flops 5368709120 | bytes 22020096 | tf_op jit(solution)/shard_map/dot_general | solution.py:173
  264.8 12.0 %add_convert_fusion = bf16[512,5120]{1,0:T(8,128)(2,1)} fusion(f32[512,5120]{1,0:T(8,128)S(1)} %fusion.3, bf16[512,1024]{0,1:T(8,128)(2,1)S(1)} %bitcast.126, bf16[2,1024,5120]{2,1,0:T(8,128)(2,1)} %all-gather.3.cloned.1.call-done), kind=kOutput, calls=%fused_computation.9 | convolution fusion | flops 5373952000 | bytes 27262976 | tf_op jit(solution)/shard_map/dot_general | solution.py:173
  277.1 128.9 %all-to-all-done.6 = bf16[8,512,1024]{1,2,0:T(8,128)(2,1)} async-done(((bf16[8,512,1024]{1,2,0:T(8,128)(2,1)}), bf16[8,512,1024]{1,2,0:T(8,128)(2,1)}, u32[]{:S(2)}, u32[]{:S(2)}) %all-to-all-start.6) | async-done | bytes 8388640 | tf_op jit(solution)/shard_map/all_to_all | solution.py:179
  407.9 35.4 %all_to_all.94 = bf16[128,8,640]{2,0,1:T(8,128)(2,1)} all-to-all(bf16[128,8,640]{2,0,1:T(8,128)(2,1)S(1)} %bitcast.108), channel_id=1, replica_groups=mesh['dp'=8,'tensor'=4] {'dp'}, dimensions={1} | all-to-all | bytes 2621440 | tf_op jit(solution)/shard_map/all_to_all | solution.py:188
  443.2 61.0 %all-gather.5.cloned.1.call-done = bf16[512,8,640]{2,0,1:T(8,128)(2,1)} async-done(((bf16[128,8,640]{2,0,1:T(8,128)(2,1)}), bf16[512,8,640]{2,0,1:T(8,128)(2,1)}) %all-gather.5.cloned.1.call-update) | async-done | bytes 5242896 | tf_op jit(solution)/shard_map/all_gather | solution.py:191
  504.2 12.3 %convert_reduce_fusion = f32[1024,640]{1,0:T(8,128)} fusion(bf16[8,512,1024]{1,2,0:T(8,128)(2,1)} %all-to-all-done.6, bf16[512,8,640]{2,0,1:T(8,128)(2,1)} %all-gather.5.cloned.1.call-done), kind=kOutput, calls=%fused_computation.3 | convolution fusion | flops 5389025280 | bytes 16252928 | tf_op jit(solution)/shard_map/csi,scd->cid/dot_general | solution.py:193
  (100 shorter events, 84.4 us)
Async XLA Ops:
  7.2 3.6 copy-start.11
  7.2 249.2 %all-gather.3.cloned.1.call-start = ((), (), s32[]{:S(2)}) async-start(), calls=%async_computation.9 | async-start | bytes 23592960 | tf_op jit(solution)/shard_map/all_gather | solution.py:172
  11.3 5.3 %copy-start.12 = (bf16[1,128,4096]{2,1,0:T(8,128)(2,1)S(1)}, bf16[1,128,4096]{2,1,0:T(8,128)(2,1)}, u32[]{:S(2)}) copy-start(bf16[1,128,4096]{2,1,0:T(8,128)(2,1)} %param.23) | copy-start | bytes 3145732
  11.4 7.0 %copy-start.17 = (s32[1,3,512]{2,0,1:T(1,128)S(1)}, s32[1,3,512]{2,0,1:T(1,128)}, u32[]{:S(2)}) copy-start(s32[1,3,512]{2,0,1:T(1,128)} %param.17) | copy-start | bytes 18436
  26.7 51.2 %all-to-all-start = ((bf16[128,4,1024]{0,2,1:T(8,128)(2,1)}), bf16[128,4,1024]{0,2,1:T(8,128)(2,1)}, u32[]{:S(2)}, u32[]{:S(2)}) async-start(bf16[128,4,1024]{0,2,1:T(8,128)(2,1)} %bitcast.5), calls=%async_computation | async-start | bytes 2097152 | tf_op jit(solution)/shard_map/all_to_all | solution.py:133
  68.1 8.7 %copy-start.7 = (bf16[128,32,64]{0,2,1:T(8,128)(2,1)S(1)}, bf16[128,32,64]{0,2,1:T(8,128)(2,1)}, u32[]{:S(2)}) copy-start(bf16[128,32,64]{0,2,1:T(8,128)(2,1)} %get-tuple-element.46) | copy-start | bytes 1572868
  68.1 8.7 %copy-start.8 = (bf16[128,32,64]{0,2,1:T(8,128)(2,1)S(1)}, bf16[128,32,64]{0,2,1:T(8,128)(2,1)}, u32[]{:S(2)}) copy-start(bf16[128,32,64]{0,2,1:T(8,128)(2,1)} %get-tuple-element.47) | copy-start | bytes 1572868
  77.9 18.4 %all-to-all-start.1 = ((bf16[128,4,1024]{0,2,1:T(8,128)(2,1)}), bf16[128,4,1024]{0,2,1:T(8,128)(2,1)}, u32[]{:S(2)}, u32[]{:S(2)}) async-start(bf16[128,4,1024]{0,2,1:T(8,128)(2,1)} %bitcast.8), calls=%async_computation.1 | async-start | bytes 2097152 | tf_op jit(solution)/shard_map/all_to_all | solution.py:134
  96.3 21.9 %all-to-all-start.3 = ((bf16[128,4,1024]{0,2,1:T(8,128)(2,1)}), bf16[128,4,1024]{0,2,1:T(8,128)(2,1)}, u32[]{:S(2)}, u32[]{:S(2)}) async-start(bf16[128,4,1024]{0,2,1:T(8,128)(2,1)} %bitcast.113), calls=%async_computation.3 | async-start | bytes 2097152 | tf_op jit(solution)/shard_map/all_to_all | solution.py:136
  100.8 7.0 %copy-start.13 = (bf16[1,128,4096]{2,1,0:T(8,128)(2,1)S(1)}, bf16[1,128,4096]{2,1,0:T(8,128)(2,1)}, u32[]{:S(2)}) copy-start(bf16[1,128,4096]{2,1,0:T(8,128)(2,1)} %param.24) | copy-start | bytes 3145732
  100.8 8.3 %copy-start.5 = (bf16[128,32,64]{0,2,1:T(8,128)(2,1)S(1)}, bf16[128,32,64]{0,2,1:T(8,128)(2,1)}, u32[]{:S(2)}) copy-start(bf16[128,32,64]{0,2,1:T(8,128)(2,1)} %get-tuple-element.14) | copy-start | bytes 1572868
  100.8 8.3 %copy-start.6 = (bf16[128,32,64]{0,2,1:T(8,128)(2,1)S(1)}, bf16[128,32,64]{0,2,1:T(8,128)(2,1)}, u32[]{:S(2)}) copy-start(bf16[128,32,64]{0,2,1:T(8,128)(2,1)} %get-tuple-element.15) | copy-start | bytes 1572868
  110.2 12.3 %copy-start.3 = (bf16[512,8,64]{2,0,1:T(8,128)(2,1)S(1)}, bf16[512,8,64]{2,0,1:T(8,128)(2,1)}, u32[]{:S(2)}) copy-start(bf16[512,8,64]{2,0,1:T(8,128)(2,1)} %get-tuple-element.7) | copy-start | bytes 1572868
  110.2 12.3 %copy-start.4 = (bf16[512,8,64]{2,0,1:T(8,128)(2,1)S(1)}, bf16[512,8,64]{2,0,1:T(8,128)(2,1)}, u32[]{:S(2)}) copy-start(bf16[512,8,64]{2,0,1:T(8,128)(2,1)} %get-tuple-element.38) | copy-start | bytes 1572868
  118.2 17.6 %all-to-all-start.4 = ((bf16[128,4,1024]{0,2,1:T(8,128)(2,1)}), bf16[128,4,1024]{0,2,1:T(8,128)(2,1)}, u32[]{:S(2)}, u32[]{:S(2)}) async-start(bf16[128,4,1024]{0,2,1:T(8,128)(2,1)} %bitcast.114), calls=%async_computation.4 | async-start | bytes 2097152 | tf_op jit(solution)/shard_map/all_to_all | solution.py:137
  125.2 3.3 copy-start.1
  130.7 12.1 %copy-start.14 = (bf16[1,128,4096]{2,1,0:T(8,128)(2,1)S(1)}, bf16[1,128,4096]{2,1,0:T(8,128)(2,1)}, u32[]{:S(2)}) copy-start(bf16[1,128,4096]{2,1,0:T(8,128)(2,1)} %param.27) | copy-start | bytes 3145732
  135.8 43.2 %all-to-all-start.2 = ((bf16[128,4,1024]{0,2,1:T(8,128)(2,1)}), bf16[128,4,1024]{0,2,1:T(8,128)(2,1)}, u32[]{:S(2)}, u32[]{:S(2)}) async-start(bf16[128,4,1024]{0,2,1:T(8,128)(2,1)} %bitcast.10), calls=%async_computation.2 | async-start | bytes 2097152 | tf_op jit(solution)/shard_map/all_to_all | solution.py:135
  179.0 32.7 %all-to-all-start.5 = ((bf16[128,4,1024]{0,2,1:T(8,128)(2,1)}), bf16[128,4,1024]{0,2,1:T(8,128)(2,1)}, u32[]{:S(2)}, u32[]{:S(2)}) async-start(bf16[128,4,1024]{0,2,1:T(8,128)(2,1)} %bitcast.112), calls=%async_computation.5 | async-start | bytes 2097152 | tf_op jit(solution)/shard_map/all_to_all | solution.py:138
  190.3 5.9 %copy-start = (f32[8,512,512]{1,2,0:T(8,128)}, f32[8,512,512]{1,2,0:T(8,128)S(1)}, u32[]{:S(2)}) copy-start(f32[8,512,512]{1,2,0:T(8,128)S(1)} %fusion.48) | copy-start | bytes 25165828
  217.0 5.2 copy-start.15
  217.0 189.0 %all-to-all-start.6 = ((bf16[8,512,1024]{1,2,0:T(8,128)(2,1)}), bf16[8,512,1024]{1,2,0:T(8,128)(2,1)}, u32[]{:S(2)}, u32[]{:S(2)}) async-start(bf16[8,512,1024]{1,2,0:T(8,128)(2,1)} %broadcast_in_dim.28), calls=%async_computation.7 | async-start | bytes 16777216 | tf_op jit(solution)/shard_map/all_to_all | solution.py:179
  222.1 183.9 %reduce-scatter.2.cloned.1.call-start = ((), (), s32[]{:S(2)}) async-start(), calls=%async_computation.10 | async-start | bytes 6553600 | tf_op jit(solution)/shard_map/reduce_scatter | solution.py:180
  234.6 10.3 %copy-start.16 = (bf16[512,8,128]{0,2,1:T(8,128)(2,1)S(1)}, bf16[512,8,128]{0,2,1:T(8,128)(2,1)}, u32[]{:S(2)}) copy-start(bf16[512,8,128]{0,2,1:T(8,128)(2,1)} %reshape.307) | copy-start | bytes 3145732
  244.8 11.6 %copy-start.9 = (bf16[512,8,128]{0,2,1:T(8,128)(2,1)S(1)}, bf16[512,8,128]{0,2,1:T(8,128)(2,1)}, u32[]{:S(2)}) copy-start(bf16[512,8,128]{0,2,1:T(8,128)(2,1)} %fusion.25) | copy-start | bytes 3145732
  276.8 129.2 %copy-start.10 = (bf16[1,128,5120]{2,1,0:T(8,128)(2,1)S(1)}, bf16[1,128,5120]{2,1,0:T(8,128)(2,1)}, u32[]{:S(2)}) copy-start(bf16[1,128,5120]{2,1,0:T(8,128)(2,1)} %param.18) | copy-start | bytes 3932164
  276.8 227.4 %all-gather.5.cloned.1.call-start = ((), (), s32[]{:S(2)}) async-start(), calls=%async_computation.11 | async-start | bytes 6553600 | tf_op jit(solution)/shard_map/all_gather | solution.py:191
  407.7 108.9 %copy-start.2 = (bf16[128,5120]{1,0:T(8,128)(2,1)}, bf16[128,5120]{1,0:T(8,128)(2,1)S(1)}, u32[]{:S(2)}) copy-start(bf16[128,5120]{1,0:T(8,128)(2,1)S(1)} %fusion.21) | copy-start | bytes 3932164
Sparse Core Ops, SparseCore 0:
  10.9 188.0 all-gather.2
  276.9 63.2 reduce-scatter.1
  443.4 60.8 all-gather.4
